TPU v7x, 32 devices: a whole 2x2x4 slice. The times are simulated.
32 devices in a mesh: task: 2 (over y), row: 4 (over z), col: 4 (over x, core).
Axes of the slice: x: 2, y: 2, z: 4, core: 2. Of those that a mesh axis runs over, the one named last changes fastest.
Arguments:
- features: bfloat16 [164, 4096], P(None, ('task', 'row', 'col')), parts along dimension 1, may hold values from -6 to 6
- rung_index: int32 [4096], P(('task', 'row', 'col')), parts along dimension 0, may hold values from 0 to 3
- w_first: bfloat16 [164, 512], replicated, may hold values from -0.5 to 0.5
- b_first: float32 [512], replicated, may hold values from -4 to 4
- w_second: bfloat16 [512, 512], replicated, may hold values from -0.25 to 0.25
- b_second: float32 [512], replicated, may hold values from -4 to 4
- w_third: bfloat16 [512, 64], replicated, may hold values from -0.25 to 0.25
- targets: float32 [16, 4096], P(None, ('task', 'row', 'col')), parts along dimension 1, may hold values from -80 to 80
- fidelity_factor: float32 [8, 4], P('task'), parts along dimension 0, may hold values from -4 to 4
- inverse_scale: float32 [2], P('task'), parts along dimension 0, may hold values from 0.02 to 0.1
- noise_var: float32 [2], P('task'), parts along dimension 0, may hold values from 0.3 to 1
Outputs:
- solution: float32 [16, 4096], P(None, ('task', 'row', 'col')), parts along dimension 1
- residual: float32 [16, 4096], P(None, ('task', 'row', 'col')), parts along dimension 1
There are 2 independent parts, one for each index of `task`. A program takes and returns all parts, laid end to end along the dimension named above; an argument that names none is the same for every part. Nothing has to cross between parts.
All inputs are finite; a program needn't handle non-finite values.
Results may differ from a plain program's by a relative error of at most 0.012.
The roundings to bfloat16 on the way count: a program that leaves them out, or rounds other values in their place, can miss the bound.
Values may be sent and summed in bfloat16 or wider, within the bound.
No kernel may reach another device: no remote copies, remote signals or barrier semaphores. Data moves between devices by JAX's collectives and lax.ppermute only.
A program may use at most 64 MiB of HBM per device.

v0:
```python
import jax
import jax.numpy as jnp
from jax import lax
from jax.sharding import PartitionSpec as P

ITERS = 2


def fidelity_matrix(fidelity_factor):
    lower = jnp.tril(fidelity_factor)
    return jnp.dot(lower, lower.T, precision=lax.Precision.HIGHEST) + 0.5 * jnp.eye(
        fidelity_factor.shape[0], dtype=jnp.float32
    )


def left_product(weights, values):
    return lax.dot_general(
        weights, values, (((0,), (0,)), ((), ())), preferred_element_type=jnp.float32
    )


def outer_gram(left_side, right_side):
    return lax.dot_general(
        left_side, right_side, (((1,), (1,)), ((), ())), precision=lax.Precision.HIGHEST
    )


def solve_spd(matrix, right_side):
    return jax.scipy.linalg.cho_solve((jnp.linalg.cholesky(matrix), True), right_side)


def block_size(total_count, largest):
    chosen = min(total_count, largest)
    while total_count % chosen != 0:
        chosen = chosen - 1
    return chosen


def one_hot_rows(rung_value, count_rungs):
    levels = jnp.arange(count_rungs, dtype=jnp.float32)
    return (rung_value.astype(jnp.float32)[:, None] == levels[None, :]).astype(jnp.float32)


def kernel_rows(
    row_embedding,
    row_squares,
    row_onehot,
    col_embedding,
    col_rung,
    direction,
    fidelity,
    inverse_scale,
):
    count_rows = row_embedding.shape[1]
    count_cols = col_embedding.shape[1]
    row_block = block_size(count_rows, 512)
    col_block = block_size(count_cols, 2048)
    col_squares = jnp.sum(jnp.square(col_embedding.astype(jnp.float32)), axis=0)
    col_fidelity = jnp.dot(
        fidelity, one_hot_rows(col_rung, fidelity.shape[0]).T, precision=lax.Precision.HIGHEST
    )

    def one_row_block(block_number):
        first_row = block_number * row_block
        rows_embedding = lax.dynamic_slice_in_dim(row_embedding, first_row, row_block, 1)
        rows_squares = lax.dynamic_slice_in_dim(row_squares, first_row, row_block, 0)
        rows_onehot = lax.dynamic_slice_in_dim(row_onehot, first_row, row_block, 0)

        def one_col_block(running, column_number):
            first_col = column_number * col_block
            cols_embedding = lax.dynamic_slice_in_dim(col_embedding, first_col, col_block, 1)
            cols_squares = lax.dynamic_slice_in_dim(col_squares, first_col, col_block, 0)
            cols_fidelity = lax.dynamic_slice_in_dim(col_fidelity, first_col, col_block, 1)
            cols_direction = lax.dynamic_slice_in_dim(direction, first_col, col_block, 1)
            inner = left_product(rows_embedding, cols_embedding)
            distance = rows_squares[:, None] + cols_squares[None, :] - 2.0 * inner
            tile_fidelity = jnp.dot(rows_onehot, cols_fidelity, precision=lax.Precision.HIGHEST)
            kernel = jnp.exp(-inverse_scale[0] * distance) * tile_fidelity
            contribution = lax.dot_general(
                cols_direction, kernel, (((1,), (1,)), ((), ())), precision=lax.Precision.HIGHEST
            )
            return (running + contribution, None)

        start_value = jnp.zeros((direction.shape[0], row_block), jnp.float32)
        result, unused = lax.scan(
            one_col_block, start_value, jnp.arange(count_cols // col_block, dtype=jnp.int32)
        )
        return result

    stacked = lax.map(one_row_block, jnp.arange(count_rows // row_block, dtype=jnp.int32))
    return jnp.transpose(stacked, (1, 0, 2)).reshape(direction.shape[0], count_rows)


def on_device(
    features,
    rung_index,
    w_first,
    b_first,
    w_second,
    b_second,
    w_third,
    targets,
    fidelity_factor,
    inverse_scale,
    noise_var,
):
    fidelity = fidelity_matrix(fidelity_factor)
    hidden_one = jax.nn.silu(left_product(w_first, features) + b_first[:, None]).astype(
        jnp.bfloat16
    )
    hidden_two = jax.nn.silu(left_product(w_second, hidden_one) + b_second[:, None]).astype(
        jnp.bfloat16
    )
    embedding = left_product(w_third, hidden_two).astype(jnp.bfloat16)
    rung_value = rung_index.astype(jnp.float32).astype(jnp.bfloat16)
    row_embedding, row_rung = (
        lax.all_gather(embedding, "col", axis=1, tiled=True),
        lax.all_gather(rung_value, "col", axis=0, tiled=True),
    )
    col_embedding, col_rung = (
        lax.all_gather(embedding, "row", axis=1, tiled=True),
        lax.all_gather(rung_value, "row", axis=0, tiled=True),
    )
    row_squares = jnp.sum(jnp.square(row_embedding.astype(jnp.float32)), axis=0)
    row_onehot = one_hot_rows(row_rung, fidelity.shape[0])
    solution = jnp.zeros_like(targets)
    residual = targets
    direction = targets
    gram = lax.psum(outer_gram(residual, residual), ("row", "col"))
    for iteration in range(ITERS):
        partial_value = kernel_rows(
            row_embedding,
            row_squares,
            row_onehot,
            col_embedding,
            col_rung,
            lax.all_gather(direction, "row", axis=1, tiled=True),
            fidelity,
            inverse_scale,
        )
        image = (
            lax.psum_scatter(partial_value, "col", scatter_dimension=1, tiled=True)
            + noise_var[0] * direction
        )
        curvature = lax.psum(outer_gram(direction, image), ("row", "col"))
        step_matrix = solve_spd(curvature, gram)
        solution = solution + jnp.dot(step_matrix.T, direction, precision=lax.Precision.HIGHEST)
        residual = residual - jnp.dot(step_matrix.T, image, precision=lax.Precision.HIGHEST)
        if iteration + 1 < ITERS:
            new_gram = lax.psum(outer_gram(residual, residual), ("row", "col"))
        if iteration + 1 < ITERS:
            update_matrix = solve_spd(gram, new_gram)
            direction = residual + jnp.dot(
                update_matrix.T, direction, precision=lax.Precision.HIGHEST
            )
            gram = new_gram
    return (solution, residual)


def solution(mesh):
    placed = (
        P(None, ("task", "row", "col")),
        P(("task", "row", "col")),
        P(),
        P(),
        P(),
        P(),
        P(),
        P(None, ("task", "row", "col")),
        P("task", None),
        P("task"),
        P("task"),
    )
    return jax.shard_map(
        on_device,
        mesh=mesh,
        in_specs=placed,
        out_specs=(P(None, ("task", "row", "col")), P(None, ("task", "row", "col"))),
        check_vma=False,
    )
```

profile of v0, /device:TPU:0, one launch (start us, length us, event | category | flops | bytes accessed | tf_op | source)
XLA Modules:
  0.0 256.6 jit_solution(4763473048253713967)
XLA Ops:
  7.2 1.3 multiply_convert_fusion.1
  9.1 13.7 %all_gather.19 = bf16[64,512]{1,0:T(8,128)(2,1)S(1)} all-gather(bf16[64,128]{1,0:T(8,128)(2,1)S(1)} %fusion.4), channel_id=1, replica_groups=mesh['task'=2,'row'=4,'col'=4] {'row'}, dimensions={1}, use_global_device_ids=true | all-gather | bytes 81920 | tf_op jit(solution)/shard_map/all_gather | solution.py:121
  22.8 5.4 %all_gather.18 = bf16[64,512]{1,0:T(8,128)(2,1)S(1)} all-gather(bf16[64,128]{1,0:T(8,128)(2,1)S(1)} %fusion.4), channel_id=1, replica_groups=mesh['task'=2,'row'=4,'col'=4] {'col'}, dimensions={1}, use_global_device_ids=true | all-gather | bytes 81920 | tf_op jit(solution)/shard_map/all_gather | solution.py:117
  28.2 9.8 %all-gather.1 = bf16[4,1,128]{2,1,0:T(2,128)(2,1)S(1)} all-gather(bf16[1,1,128]{2,1,0:T(2,128)(2,1)S(1)} %convert_bitcast_fusion), channel_id=1, replica_groups=mesh['task'=2,'row'=4,'col'=4] {'row'}, dimensions={0}, use_global_device_ids=true | all-gather | bytes 1280 | tf_op jit(solution)/shard_map/all_gather | solution.py:122
  38.0 5.0 %all-gather = bf16[4,1,128]{2,1,0:T(2,128)(2,1)S(1)} all-gather(bf16[1,1,128]{2,1,0:T(2,128)(2,1)S(1)} %convert_bitcast_fusion), channel_id=1, replica_groups=mesh['task'=2,'row'=4,'col'=4] {'col'}, dimensions={0}, use_global_device_ids=true | all-gather | bytes 1280 | tf_op jit(solution)/shard_map/all_gather | solution.py:118
  44.5 13.1 %all_gather.22 = f32[16,512]{1,0:T(8,128)S(1)} all-gather(f32[16,128]{1,0:T(8,128)S(1)} %copy-done.1), channel_id=1, replica_groups=mesh['task'=2,'row'=4,'col'=4] {'row'}, dimensions={1}, use_global_device_ids=true | all-gather | bytes 40960 | tf_op jit(solution)/shard_map/all_gather | solution.py:137
  59.0 1.6 convolution_bitcast_fusion
  61.5 17.0 %reduce-scatter.3.cloned.1.call-done = f32[16,128]{1,0:T(8,128)} async-done(((f32[16,512]{1,0:T(8,128)}), f32[16,128]{1,0:T(8,128)}) %reduce-scatter.3.cloned.1.call-update) | async-done | bytes 8208 | tf_op jit(solution)/shard_map/reduce_scatter | solution.py:142
  78.5 0.8 convolution_bitcast_fusion.1
  79.3 59.7 %all-reduce = (f32[16,16]{0,1:T(8,128)S(1)}, f32[16,16]{0,1:T(8,128)S(1)}) all-reduce(f32[16,16]{0,1:T(8,128)S(1)} %fusion.37, f32[16,16]{0,1:T(8,128)S(1)} %convolution_bitcast_fusion.1), channel_id=1, replica_groups=mesh['task'=2,'row'=4,'col'=4] {'row','col'}, use_global_device_ids=true, to_apply=%region_6.8 | all-reduce | flops 512 | bytes 4096 | tf_op jit(solution)/shard_map/psum | solution.py:129
  139.2 1.5 cholesky.70
  142.0 1.2 custom-call.10
  143.2 1.5 cholesky.59
  146.0 1.2 custom-call.9
  148.5 30.0 %psum.30 = f32[16,16]{1,0:T(8,128)S(1)} all-reduce(f32[16,16]{1,0:T(8,128)S(1)} %fusion.39), channel_id=1, replica_groups=mesh['task'=2,'row'=4,'col'=4] {'row','col'}, use_global_device_ids=true, to_apply=%region_7.10 | all-reduce | flops 256 | bytes 2048 | tf_op jit(solution)/shard_map/psum | solution.py:150
  179.0 13.1 %all_gather.23 = f32[16,512]{1,0:T(8,128)S(1)} all-gather(f32[16,128]{1,0:T(8,128)S(1)} %convolution_add_fusion.3), channel_id=1, replica_groups=mesh['task'=2,'row'=4,'col'=4] {'row'}, dimensions={1}, use_global_device_ids=true | all-gather | bytes 40960 | tf_op jit(solution)/shard_map/all_gather | solution.py:137
  192.1 1.6 fusion.40
  193.9 16.7 %reduce-scatter.5.cloned.1.call-done = f32[16,128]{1,0:T(8,128)} async-done(((f32[16,512]{1,0:T(8,128)}), f32[16,128]{1,0:T(8,128)}) %reduce-scatter.5.cloned.1.call-update) | async-done | bytes 8208 | tf_op jit(solution)/shard_map/reduce_scatter | solution.py:142
  210.7 0.8 fusion.28
  211.5 32.2 %psum.31 = f32[16,16]{0,1:T(8,128)S(1)} all-reduce(f32[16,16]{0,1:T(8,128)S(1)} %fusion.28), channel_id=1, replica_groups=mesh['task'=2,'row'=4,'col'=4] {'row','col'}, use_global_device_ids=true, to_apply=%region_9.12 | all-reduce | flops 256 | bytes 2048 | tf_op jit(solution)/shard_map/psum | solution.py:145
  243.8 1.5 cholesky.81
  246.6 1.2 custom-call.11
  248.1 0.8 convolution_add_fusion.2
  249.0 0.8 convolution_subtract_fusion
  (55 shorter events, 9.4 us)
Async XLA Ops:
  7.2 1.4 copy-start
  7.2 1.4 copy-start.5
  7.2 1.4 copy-start.4
  7.2 71.3 %reduce-scatter.3.cloned.1.call-start = ((), (), s32[]{:S(2)}) async-start(), calls=%async_computation.2 | async-start | bytes 40960 | tf_op jit(solution)/shard_map/reduce_scatter | solution.py:142
  22.8 5.4 %copy-start.7 = (s32[128]{0:T(128)S(1)}, s32[128]{0:T(128)}, u32[]{:S(2)}) copy-start(s32[128]{0:T(128)} %param.15) | copy-start | bytes 1540
  43.1 0.7 copy-start.6
  43.8 0.7 copy-start.1
  60.6 150.1 %reduce-scatter.5.cloned.1.call-start = ((), (), s32[]{:S(2)}) async-start(), calls=%async_computation.3 | async-start | bytes 40960 | tf_op jit(solution)/shard_map/reduce_scatter | solution.py:142
  147.4 0.7 copy-start.2
  248.1 0.8 copy-start.3
Sparse Core Ops, SparseCore 0:
  60.7 17.7 reduce-scatter.2
  193.9 16.7 reduce-scatter.4
where the time goes:
time: 257 us
  blocking collectives  182 us (71%)
  waiting for transfers between devices  33.8 us (13%)
  between operations  15.5 us (6%)
  other arithmetic  12.1 us (5%)
  matrix products  11.6 us (5%)
    psum x1, blocking collectives, on_device(): gram = lax.psum(outer_gram(residual, residual), ('row', 'col'))  59.7 us
    reduce_scatter x2, waiting for transfers between devices, on_device(): lax.psum_scatter(partial_value, 'col', scatter_dimension=1, tiled=True)  33.8 us
    psum x1, blocking collectives, on_device(): curvature = lax.psum(outer_gram(direction, image), ('row', 'col'))  32.2 us
    psum x1, blocking collectives, on_device(): new_gram = lax.psum(outer_gram(residual, residual), ('row', 'col'))  30 us
    all_gather x2, blocking collectives, on_device(): lax.all_gather(direction, 'row', axis=1, tiled=True)  26.2 us
    all_gather x1, blocking collectives, on_device(): lax.all_gather(embedding, 'row', axis=1, tiled=True)  13.7 us
    all_gather x1, blocking collectives, on_device(): lax.all_gather(rung_value, 'row', axis=0, tiled=True)  9.84 us
    another operation x9, other arithmetic, solve_spd(): jnp.linalg.cholesky(matrix)  6.39 us
  transfers between devices with their start and end apart: 2, of which 2 were waited for; matrix products, arithmetic and copies ran while one was open for 0% of the time, Pallas kernels for 0%

commit v1 on v0

--- a/solution.py
+++ b/solution.py
@@ -126,7 +126,11 @@
     solution = jnp.zeros_like(targets)
     residual = targets
     direction = targets
-    gram = lax.psum(outer_gram(residual, residual), ("row", "col"))
+
+    def spans_make(sheet):
+        return jnp.sum(lax.all_gather(sheet, ("row", "col")), axis=0)
+
+    gram = spans_make(outer_gram(residual, residual))
     for iteration in range(ITERS):
         partial_value = kernel_rows(
             row_embedding,

time: 257 us -> 230 us (0.89)
  waiting for transfers between devices: 33.8 us -> 16.8 us
  blocking collectives: 182 us -> 172 us
    psum x1 -> x0, blocking collectives: 59.7 us -> none  [on_device(): gram = lax.psum(outer_gram(residual, residual), ('row', 'col'))]
    psum x1 -> x2, blocking collectives: 32.2 us -> 62.7 us  [on_device(): curvature = lax.psum(outer_gram(direction, image), ('row', 'col'))]
    all_gather x0 -> x1, blocking collectives: none -> 18.9 us  [spans_make(): return jnp.sum(lax.all_gather(sheet, ('row', 'col')), axis=0)]
    reduce_scatter x2, waiting for transfers between devices: 33.8 us -> 16.8 us  [on_device(): lax.psum_scatter(partial_value, 'col', scatter_dimension=1, tiled=True)]
  transfers between devices with their start and end apart: 2 -> 2, of which waited for: 2 -> 1; matrix products, arithmetic and copies ran while one was open for 0% -> 2% of each run, Pallas kernels for 0% -> 0%
where the time goes in v1:
time: 230 us; the launch traced here: 229 us
  blocking collectives  172 us (75%)
  waiting for transfers between devices  16.8 us (7%)
  between operations  15.5 us (7%)
  other arithmetic  12.1 us (5%)
  matrix products  11.6 us (5%)
    psum x2, blocking collectives, on_device(): curvature = lax.psum(outer_gram(direction, image), ('row', 'col'))  62.7 us
    psum x1, blocking collectives, on_device(): new_gram = lax.psum(outer_gram(residual, residual), ('row', 'col'))  30 us
    all_gather x2, blocking collectives, on_device(): lax.all_gather(direction, 'row', axis=1, tiled=True)  26.2 us
    all_gather x1, blocking collectives, spans_make(): return jnp.sum(lax.all_gather(sheet, ('row', 'col')), axis=0)  18.9 us
    reduce_scatter x2, waiting for transfers between devices, on_device(): lax.psum_scatter(partial_value, 'col', scatter_dimension=1, tiled=True)  16.8 us
    all_gather x1, blocking collectives, on_device(): lax.all_gather(embedding, 'row', axis=1, tiled=True)  12.9 us
    all_gather x1, blocking collectives, on_device(): lax.all_gather(rung_value, 'row', axis=0, tiled=True)  9.83 us
    another operation x9, other arithmetic, solve_spd(): jnp.linalg.cholesky(matrix)  6.39 us
  transfers between devices with their start and end apart: 2, of which 1 were waited for; matrix products, arithmetic and copies ran while one was open for 2% of the time, Pallas kernels for 0%

profile of v1, /device:TPU:0, one launch (start us, length us, event | category | flops | bytes accessed | tf_op | source)
XLA Modules:
  0.0 229.3 jit_solution(7015439750366681037)
XLA Ops:
  7.2 1.3 multiply_convert_fusion.1
  9.1 6.2 %all_gather.24 = bf16[64,512]{1,0:T(8,128)(2,1)S(1)} all-gather(bf16[64,128]{1,0:T(8,128)(2,1)S(1)} %fusion.4), channel_id=1, replica_groups=mesh['task'=2,'row'=4,'col'=4] {'col'}, dimensions={1}, use_global_device_ids=true | all-gather | bytes 81920 | tf_op jit(solution)/shard_map/all_gather | solution.py:117
  15.3 12.9 %all_gather.25 = bf16[64,512]{1,0:T(8,128)(2,1)S(1)} all-gather(bf16[64,128]{1,0:T(8,128)(2,1)S(1)} %fusion.4), channel_id=1, replica_groups=mesh['task'=2,'row'=4,'col'=4] {'row'}, dimensions={1}, use_global_device_ids=true | all-gather | bytes 81920 | tf_op jit(solution)/shard_map/all_gather | solution.py:121
  28.2 9.8 %all-gather.2 = bf16[4,1,128]{2,1,0:T(2,128)(2,1)S(1)} all-gather(bf16[1,1,128]{2,1,0:T(2,128)(2,1)S(1)} %convert_bitcast_fusion), channel_id=1, replica_groups=mesh['task'=2,'row'=4,'col'=4] {'row'}, dimensions={0}, use_global_device_ids=true | all-gather | bytes 1280 | tf_op jit(solution)/shard_map/all_gather | solution.py:122
  38.0 5.0 %all-gather.1 = bf16[4,1,128]{2,1,0:T(2,128)(2,1)S(1)} all-gather(bf16[1,1,128]{2,1,0:T(2,128)(2,1)S(1)} %convert_bitcast_fusion), channel_id=1, replica_groups=mesh['task'=2,'row'=4,'col'=4] {'col'}, dimensions={0}, use_global_device_ids=true | all-gather | bytes 1280 | tf_op jit(solution)/shard_map/all_gather | solution.py:118
  44.5 13.1 %all_gather.28 = f32[16,512]{1,0:T(8,128)S(1)} all-gather(f32[16,128]{1,0:T(8,128)S(1)} %copy-done.1), channel_id=1, replica_groups=mesh['task'=2,'row'=4,'col'=4] {'row'}, dimensions={1}, use_global_device_ids=true | all-gather | bytes 40960 | tf_op jit(solution)/shard_map/all_gather | solution.py:141
  59.0 1.6 convolution_bitcast_fusion
  60.8 18.9 %all-gather = f32[256,16]{1,0:T(8,128)S(1)} all-gather(f32[16,16]{1,0:T(8,128)S(1)} %fusion.37), channel_id=2, replica_groups=mesh['task'=2,'row'=4,'col'=4] {'row','col'}, dimensions={0}, use_global_device_ids=true | all-gather | bytes 17408 | tf_op jit(solution)/shard_map/all_gather | solution.py:131
  79.8 1.5 cholesky.70
  83.2 1.2 custom-call.10
  84.5 0.8 convolution_bitcast_fusion.1
  85.3 30.5 %psum.21 = f32[16,16]{0,1:T(8,128)S(1)} all-reduce(f32[16,16]{0,1:T(8,128)S(1)} %convolution_bitcast_fusion.1), channel_id=1, replica_groups=mesh['task'=2,'row'=4,'col'=4] {'row','col'}, use_global_device_ids=true, to_apply=%region_3.4 | all-reduce | flops 256 | bytes 2048 | tf_op jit(solution)/shard_map/psum | solution.py:149
  115.9 1.5 cholesky.59
  118.6 1.2 custom-call.9
  121.1 30.0 %psum.22 = f32[16,16]{1,0:T(8,128)S(1)} all-reduce(f32[16,16]{1,0:T(8,128)S(1)} %fusion.39), channel_id=1, replica_groups=mesh['task'=2,'row'=4,'col'=4] {'row','col'}, use_global_device_ids=true, to_apply=%region_7.10 | all-reduce | flops 256 | bytes 2048 | tf_op jit(solution)/shard_map/psum | solution.py:154
  151.7 13.1 %all_gather.31 = f32[16,512]{1,0:T(8,128)S(1)} all-gather(f32[16,128]{1,0:T(8,128)S(1)} %convolution_add_fusion.3), channel_id=1, replica_groups=mesh['task'=2,'row'=4,'col'=4] {'row'}, dimensions={1}, use_global_device_ids=true | all-gather | bytes 40960 | tf_op jit(solution)/shard_map/all_gather | solution.py:141
  164.8 1.6 fusion.40
  166.6 16.8 %reduce-scatter.5.cloned.1.call-done = f32[16,128]{1,0:T(8,128)} async-done(((f32[16,512]{1,0:T(8,128)}), f32[16,128]{1,0:T(8,128)}) %reduce-scatter.5.cloned.1.call-update) | async-done | bytes 8208 | tf_op jit(solution)/shard_map/reduce_scatter | solution.py:146
  183.4 0.8 fusion.28
  184.2 32.2 %psum.23 = f32[16,16]{0,1:T(8,128)S(1)} all-reduce(f32[16,16]{0,1:T(8,128)S(1)} %fusion.28), channel_id=1, replica_groups=mesh['task'=2,'row'=4,'col'=4] {'row','col'}, use_global_device_ids=true, to_apply=%region_9.12 | all-reduce | flops 256 | bytes 2048 | tf_op jit(solution)/shard_map/psum | solution.py:149
  216.5 1.5 cholesky.81
  219.3 1.2 custom-call.11
  220.8 0.8 convolution_add_fusion.2
  221.7 0.8 convolution_subtract_fusion
  (58 shorter events, 9.4 us)
Async XLA Ops:
  7.2 1.4 copy-start
  7.2 1.4 copy-start.4
  7.2 1.4 copy-start.5
  7.2 77.3 %reduce-scatter.3.cloned.1.call-start = ((), (), s32[]{:S(2)}) async-start(), calls=%async_computation.2 | async-start | bytes 40960 | tf_op jit(solution)/shard_map/reduce_scatter | solution.py:146
  15.3 12.9 %copy-start.7 = (s32[128]{0:T(128)S(1)}, s32[128]{0:T(128)}, u32[]{:S(2)}) copy-start(s32[128]{0:T(128)} %param.15) | copy-start | bytes 1540
  43.1 0.7 copy-start.6
  43.8 0.7 copy-start.1
  60.6 122.8 %reduce-scatter.5.cloned.1.call-start = ((), (), s32[]{:S(2)}) async-start(), calls=%async_computation.3 | async-start | bytes 40960 | tf_op jit(solution)/shard_map/reduce_scatter | solution.py:146
  120.1 0.7 copy-start.2
  220.8 0.8 copy-start.3
Sparse Core Ops, SparseCore 0:
  60.7 17.7 reduce-scatter.2
  166.5 16.8 reduce-scatter.4
